TPU v7x, 128 devices: a whole 4x4x4 slice. The times are simulated.
128 devices in a mesh: lead: 32 (over x, y_lo, z), sub: 4 (over y_hi, core).
Axes of the slice: x: 4, y: 4 (y_hi: 2, y_lo: 2; y = y_hi * 2 + y_lo), z: 4, core: 2. Of those that a mesh axis runs over, the one named last changes fastest.
Arguments:
- state: float32 [67108864], P(('lead', 'sub')), may hold values from 0.135 to 67, as said below
- couplings: float32 [2, 16], replicated, may hold values from 0.25 to 16, as said below
Outputs:
- evolved: float32 [67108864], P(('lead', 'sub'))
- log_growth: float32 [], replicated
Inputs may be any that keep to these rules, and one draw needn't show every extreme that they name: `state`: every entry is positive. `couplings`: row 0 lies between 8 and 16, row 1 between 0.25 and 0.5.
All inputs are finite; a program needn't handle non-finite values.
Results may differ from a plain program's by a relative error of at most 0.0003.
Values sent between devices are 32-bit elements; how exact they have to be, the bound alone decides.
No kernel may reach another device: no remote copies, remote signals or barrier semaphores. Data moves between devices by JAX's collectives and lax.ppermute only.
A program may use at most 64 MiB of HBM per device.

v0:
```python
import jax
import jax.numpy as jnp
from jax import lax
from jax.sharding import PartitionSpec as P

BLOCK = 4
WINDOWS = 2
AXES = ("lead", "sub")


def block_kernel(vertical, horizontal, spread):
    position = jnp.arange(spread, dtype=jnp.int32)
    digits = [position // 4 ** (BLOCK - 1 - level) % 4 for level in range(BLOCK)]
    kernel = jnp.ones((spread, spread), jnp.float32)
    for level in range(BLOCK):
        same_spin = (digits[level][:, None] == digits[level][None, :]).astype(jnp.float32)
        kernel = kernel * (1.0 + vertical[level] * same_spin)
    for level in range(1, BLOCK):
        chained = (digits[level - 1] == digits[level]).astype(jnp.float32)
        kernel = kernel * (1.0 + horizontal[level] * chained)[None, :]
    labels = jnp.arange(4, dtype=jnp.int32)
    first_bond = 1.0 + horizontal[0] * (labels[:, None] == labels[None, :]).astype(jnp.float32)
    return (kernel, first_bond)


def multiply(matrix, kernel):
    return lax.dot_general(
        matrix,
        kernel,
        (((0,), (0,)), ((), ())),
        precision=lax.Precision.HIGHEST,
        preferred_element_type=jnp.float32,
    )


def contract(flat, kernel, first_bond, spread):
    result = multiply(flat.reshape(spread, -1), kernel)
    bonded = result.reshape(-1, 4, 4, spread // 4) * first_bond[None, :, :, None]
    return bonded.reshape(-1)


def exchange(flat, devices, minor, extra=None):
    shaped = flat.reshape(-1, devices, minor)
    rows = jnp.transpose(shaped, (1, 0, 2)).reshape(devices, -1)
    if extra is not None:
        rows = jnp.concatenate([rows, extra], axis=1)
    return lax.all_to_all(rows, AXES, 0, 0, tiled=True)


def shards(state, couplings):
    lead_count = lax.axis_size("lead")
    sub_count = lax.axis_size("sub")
    devices = lead_count * sub_count
    me = lax.axis_index("lead") * sub_count + lax.axis_index("sub")
    spread = 4**BLOCK
    whole_count = state.shape[0] * devices
    minor = 4**5 // devices
    kernels = []
    for block in range(2 * WINDOWS):
        first_site = block * BLOCK
        kernels.append(
            block_kernel(
                couplings[0, first_site : first_site + BLOCK],
                couplings[1, first_site : first_site + BLOCK],
                spread,
            )
        )

    current = exchange(state, devices, minor).reshape(-1)
    current = contract(current, *kernels[0], spread)
    current = contract(current, *kernels[1], spread)

    kernel3, bond3 = kernels[2]
    kernel4, bond4 = kernels[3]
    tail = kernel4.reshape(spread, 4, spread // 4).sum(axis=2)
    tail = lax.dot_general(tail, bond4, (((1,), (1,)), ((), ())), precision=lax.Precision.HIGHEST)
    column = jnp.arange(spread, dtype=jnp.int32)
    gather = bond3[:, column // (spread // 4)].T[:, None, :] * tail[:, column % 4].T[:, :, None]
    per_row = spread // devices
    rows = lax.dynamic_slice_in_dim(kernel3, me * per_row, per_row, axis=0)
    weight = lax.dot_general(
        rows, gather.reshape(spread, -1), (((1,), (0,)), ((), ())), precision=lax.Precision.HIGHEST
    ).reshape(per_row, spread, 1, 4)
    middle_part = jnp.sum(current)
    final_part = jnp.sum(current.reshape(per_row, spread, -1, 4) * weight)

    extra = jnp.zeros((devices, 128), jnp.float32)
    extra = extra.at[:, 0].set(middle_part).at[:, 1].set(final_part)
    received = exchange(current, devices, minor, extra)
    middle_total = jnp.sum(received[:, -128])
    final_total = jnp.sum(received[:, -127])
    current = received[:, :-128].reshape(-1)

    current = contract(current, *kernels[2], spread)
    current = contract(current, *kernels[3], spread)

    middle_mean = middle_total / whole_count
    last_mean = final_total / middle_mean / whole_count
    current = current / (middle_mean * last_mean)
    growth = jnp.log(middle_mean) + jnp.log(last_mean)
    return (current, growth)


def solution(mesh):
    in_specs = (P(AXES), P())
    out_specs = (P(AXES), P())
    return jax.shard_map(shards, mesh=mesh, in_specs=in_specs, out_specs=out_specs, check_vma=False)
```

profile of v0, /device:TPU:1, one launch (start us, length us, event | category | flops | bytes accessed | tf_op | source)
XLA Modules:
  0.0 233.2 jit_solution(3658218277179936251)
XLA Ops:
  0.6 22.2 %reshape.830 = f32[512,128,8]{2,1,0:T(8,128)} reshape(f32[524288]{0:T(1024)} %param.6) | data formatting | bytes 4194304 | tf_op jit(solution)/shard_map/reshape | solution.py:43
  22.8 17.4 %copy.65 = f32[128,512,8]{0,2,1:T(8,128)S(1)} copy(f32[128,512,8]{2,0,1:T(8,128)} %bitcast.76) | data formatting | bytes 4194304 | tf_op jit(solution)/shard_map/transpose | solution.py:44
  40.2 4.1 %copy.66 = f32[128,1,4096]{2,1,0:T(1,128)} copy(f32[128,1,4096]{0,2,1:T(8,128)S(1)} %bitcast.82) | data formatting | bytes 4194304 | tf_op jit(solution)/shard_map/all_to_all | solution.py:47
  44.3 11.9 %all-to-all-start = ((f32[128,1,4096]{2,1,0:T(1,128)}), f32[128,1,4096]{2,1,0:T(1,128)}, u32[]{:S(2)}, u32[]{:S(2)}) async-start(f32[128,1,4096]{2,1,0:T(1,128)} %copy.66), calls=%async_computation | async-start | bytes 4194304 | tf_op jit(solution)/shard_map/all_to_all | solution.py:47
  59.6 2.8 %multiply_reduce_fusion.1 = f32[256,4]{0,1:T(4,128)S(1)} fusion(f32[4,64]{1,0:T(4,128)S(1)} %get-tuple-element.77, f32[4,64]{1,0:T(4,128)S(1)} %get-tuple-element.78, f32[4,64]{1,0:T(4,128)S(1)} %select_add_fusion.6, f32[]{:T(128)} %bitcast.39, s32[4,64]{1,0:T(4,128)S(1)} %get-tuple-element.73, s32[256]{0:T(256)S(1)} %get-tuple-element.65, f32[]{:T(128)} %bitcast.38, ...), kind=kLoop, calls=%fused_computation.81 | loop fusion | flops 1244160 | bytes 15376 | tf_op jit(solution)/shard_map/reduce_sum | solution.py:75
  72.3 1.9 mul.703
  74.2 2.9 %mul.704 = f32[512,4,4,64]{0,3,2,1:T(8,128)S(1)} reshape(f32[2,256,256,4]{1,0,3,2:T(2,128)} %mul.703) | data formatting | bytes 4194304 | tf_op jit(solution)/shard_map/mul | solution.py:85
  77.9 2.5 %mul.617 = f32[512,4,4,64]{3,2,1,0:T(4,128)} broadcast(f32[4,4]{1,0:T(4,128)S(1)} %copy.68), dimensions={1,2} | broadcast | bytes 2097216 | tf_op jit(solution)/shard_map/mul | solution.py:38
  80.4 5.6 %mul.618 = f32[256,2048]{1,0:T(8,128)} reshape(f32[512,4,4,64]{3,2,1,0:T(4,128)} %mul.617) | data formatting | bytes 4194304 | tf_op jit(solution)/shard_map/mul | solution.py:38
  91.8 8.0 %reduce.18 = f32[128,4096]{1,0:T(8,128)} reduce(f32[128,1,4096]{2,1,0:T(1,128)} %all-to-all-done, f32[]{:T(128)} %constant.403), dimensions={1}, to_apply=%all_to_all.15.reduce_sub_computation | reduce | bytes 4194308 | tf_op jit(solution)/shard_map/all_to_all | solution.py:47
  99.8 2.8 %reshape_reshape.14 = f32[256,2048]{1,0:T(8,128)} reshape(f32[128,4096]{1,0:T(8,128)} %reduce.18) | data formatting | bytes 4194304 | tf_op jit(solution)/shard_map/reshape;reshape | solution.py:37
  102.6 7.5 %convolution_bitcast_fusion = f32[2048,256]{0,1:T(8,128)} fusion(f32[256,2048]{1,0:T(8,128)} %reshape_reshape.14, f32[256]{0:T(256)S(1)} %get-tuple-element.71, f32[256]{0:T(256)S(1)} %get-tuple-element.72, f32[256]{0:T(256)S(1)} %select_add_fusion.18, f32[]{:T(128)} %bitcast.3, f32[]{:T(128)} %bitcast.2, s32[256]{0:T(256)S(1)} %get-tuple-element.66, ...), kind=kOutput, calls=%fused_computation.2 | convolution fusion | flops 1611792384 | bytes 4201488 | tf_op jit(solution)/shard_map/dot_general | solution.py:27
  110.1 2.9 %copy.67 = f32[2048,256]{1,0:T(8,128)} copy(f32[2048,256]{0,1:T(8,128)} %convolution_bitcast_fusion) | data formatting | bytes 4194304 | tf_op jit(solution)/shard_map/dot_general | solution.py:27
  113.0 2.7 %reshape.831 = f32[256,2048]{1,0:T(8,128)} reshape(f32[2048,256]{1,0:T(8,128)} %copy.67) | data formatting | bytes 4194304 | tf_op jit(solution)/shard_map/reshape | solution.py:38
  115.7 3.9 %multiply_bitcast_fusion = f32[2048,256]{0,1:T(8,128)} fusion(f32[256,2048]{1,0:T(8,128)} %reshape.831, f32[256,2048]{1,0:T(8,128)} %mul.618), kind=kLoop, calls=%fused_computation.13 | loop fusion | flops 524288 | bytes 6291456 | tf_op jit(solution)/shard_map/dot_general | solution.py:27
  119.6 2.9 %copy.69 = f32[2048,256]{1,0:T(8,128)} copy(f32[2048,256]{0,1:T(8,128)} %multiply_bitcast_fusion) | data formatting | bytes 4194304 | tf_op jit(solution)/shard_map/dot_general | solution.py:27
  122.5 2.8 %dot_general.37 = f32[512,4,256]{2,1,0:T(4,128)} reshape(f32[2048,256]{1,0:T(8,128)} %copy.69) | data formatting | bytes 4194304 | tf_op jit(solution)/shard_map/dot_general | solution.py:27
  125.4 8.6 %multiply_reduce_fusion = (f32[]{:T(128)}, f32[]{:T(128)}, f32[512,4,4,64]{0,3,2,1:T(8,128)}) fusion(f32[512,4,4,64]{0,3,2,1:T(8,128)S(1)} %mul.704, f32[4,4]{1,0:T(4,128)S(1)} %copy.71, f32[4,64]{1,0:T(4,128)S(1)} %get-tuple-element.79, f32[4,64]{1,0:T(4,128)S(1)} %get-tuple-element.80, f32[4,64]{1,0:T(4,128)S(1)} %select_add_fusion.11, f32[]{:T(128)} %bitcast.16, ...), kind=kOutput, calls=%fused_computation.12 | convolution fusion | flops 1613889536 | bytes 6302808 | tf_op jit(solution)/shard_map/dot_general | solution.py:27
  134.0 3.1 %copy.72 = f32[512,128,8]{1,2,0:T(8,128)} copy(f32[512,128,8]{0,2,1:T(8,128)} %bitcast.78) | data formatting | bytes 4194304 | tf_op jit(solution)/shard_map/reshape;reshape | solution.py:43
  141.4 4.2 %copy.76 = f32[128,1,4224]{2,1,0:T(1,128)} copy(f32[128,1,4224]{0,2,1:T(8,128)S(1)} %maximum_bitcast_fusion) | data formatting | bytes 4325376 | tf_op jit(solution)/shard_map/all_to_all | solution.py:47
  145.6 10.2 %all-to-all-start.1 = ((f32[128,1,4224]{2,1,0:T(1,128)}), f32[128,1,4224]{2,1,0:T(1,128)}, u32[]{:S(2)}, u32[]{:S(2)}) async-start(f32[128,1,4224]{2,1,0:T(1,128)} %copy.76), calls=%async_computation.1 | async-start | bytes 4325376 | tf_op jit(solution)/shard_map/all_to_all | solution.py:47
  158.4 27.3 %all-to-all-done.1 = f32[128,1,4224]{2,1,0:T(1,128)} async-done(((f32[128,1,4224]{2,1,0:T(1,128)}), f32[128,1,4224]{2,1,0:T(1,128)}, u32[]{:S(2)}, u32[]{:S(2)}) %all-to-all-start.1) | async-done | bytes 2162720 | tf_op jit(solution)/shard_map/all_to_all | solution.py:47
  193.4 1.8 copy.77
  195.3 2.9 %dot_general.43 = f32[512,4,256]{2,1,0:T(4,128)} reshape(f32[2048,256]{1,0:T(8,128)} %copy.77) | data formatting | bytes 4194304 | tf_op jit(solution)/shard_map/dot_general | solution.py:27
  198.1 6.2 %fusion.9 = f32[512,4,4,64]{0,3,2,1:T(8,128)S(1)} fusion(f32[512,4,256,1]{2,1,0,3:T(4,128)} %bitcast.79, f32[4,4]{1,0:T(4,128)S(1)} %copy.79, f32[4,64]{1,0:T(4,128)S(1)} %get-tuple-element.81, f32[4,64]{1,0:T(4,128)S(1)} %get-tuple-element.82, f32[4,64]{1,0:T(4,128)S(1)} %select_add_fusion.2, f32[]{:T(128)} %bitcast.29, f32[]{:T(128)} %bitcast.28, ...), kind=kOutput, calls=%fused_computation.15 | convolution fusion | flops 1612316672 | bytes 4205648 | tf_op jit(solution)/shard_map/dot_general | solution.py:27
  204.4 3.4 %copy.80 = f32[512,4,4,64]{3,2,1,0:T(4,128)} copy(f32[512,4,4,64]{0,3,2,1:T(8,128)S(1)} %fusion.9) | data formatting | bytes 4194304 | tf_op jit(solution)/shard_map/mul | solution.py:38
  207.8 4.5 %reshape_reshape.17 = f32[256,2048]{1,0:T(8,128)S(1)} reshape(f32[512,4,4,64]{3,2,1,0:T(4,128)} %copy.80) | data formatting | bytes 4194304 | tf_op jit(solution)/shard_map/reshape;reshape | solution.py:37
  212.4 1.8 copy.81
  214.2 2.9 %dot_general.46 = f32[512,4,256]{2,1,0:T(4,128)} reshape(f32[2048,256]{1,0:T(8,128)} %copy.81) | data formatting | bytes 4194304 | tf_op jit(solution)/shard_map/dot_general | solution.py:27
  217.1 6.4 %multiply_divide_fusion = f32[512,4,4,64]{0,3,2,1:T(8,128)S(1)} fusion(f32[512,4,256,1]{2,1,0,3:T(4,128)} %bitcast.87, f32[]{:T(128)S(6)} %mul.751, f32[4,4]{1,0:T(4,128)S(1)} %copy.83, f32[4,64]{1,0:T(4,128)S(1)} %get-tuple-element.77, f32[4,64]{1,0:T(4,128)S(1)} %get-tuple-element.78, f32[4,64]{1,0:T(4,128)S(1)} %select_add_fusion.6, f32[]{:T(128)} %bitcast.39, ...), kind=kOutput, calls=%fused_computation.11 | convolution fusion | flops 1612840960 | bytes 4205652 | tf_op jit(solution)/shard_map/dot_general | solution.py:27
  223.5 3.4 %copy.84 = f32[512,4,4,64]{3,2,1,0:T(4,128)} copy(f32[512,4,4,64]{0,3,2,1:T(8,128)S(1)} %multiply_divide_fusion) | data formatting | bytes 4194304 | tf_op jit(solution)/shard_map/div | solution.py:99
  226.9 5.1 %div.192 = f32[524288]{0:T(1024)} reshape(f32[512,4,4,64]{3,2,1,0:T(4,128)} %copy.84) | data formatting | bytes 4194304 | tf_op jit(solution)/shard_map/div | solution.py:99
  (54 shorter events, 29.8 us)
Async XLA Ops:
  44.3 12.0 %copy-start = (f32[2,16]{1,0:T(2,128)S(1)}, f32[2,16]{1,0:T(2,128)}, u32[]{:S(2)}) copy-start(f32[2,16]{1,0:T(2,128)} %param.7) | copy-start | bytes 388
  44.3 47.5 %all-to-all-start = ((f32[128,1,4096]{2,1,0:T(1,128)}), f32[128,1,4096]{2,1,0:T(1,128)}, u32[]{:S(2)}, u32[]{:S(2)}) async-start(f32[128,1,4096]{2,1,0:T(1,128)} %copy.66), calls=%async_computation | async-start | bytes 4194304 | tf_op jit(solution)/shard_map/all_to_all | solution.py:47
  145.6 40.1 %all-to-all-start.1 = ((f32[128,1,4224]{2,1,0:T(1,128)}), f32[128,1,4224]{2,1,0:T(1,128)}, u32[]{:S(2)}, u32[]{:S(2)}) async-start(f32[128,1,4224]{2,1,0:T(1,128)} %copy.76), calls=%async_computation.1 | async-start | bytes 4325376 | tf_op jit(solution)/shard_map/all_to_all | solution.py:47
where the time goes:
time: 235 us; the launch traced here: 233 us
  local copies, waits for them, and re-layouts  113 us (48%)
  other arithmetic  32.6 us (14%)
  matrix products  31.2 us (13%)
  waiting for transfers between devices  27.3 us (12%)
  starting transfers between devices  22.1 us (9%)
  between operations  6.56 us (3%)
    dot_general x4, matrix products, multiply(): lax.dot_general(matrix, kernel, (((0,), (0,)), ((), ())), precision=lax.P...  28.8 us
    all_to_all x2, waiting for transfers between devices, exchange(): return lax.all_to_all(rows, AXES, 0, 0, tiled=True)  27.3 us
    reshape x1, local copies, waits for them, and re-layouts, exchange(): shaped = flat.reshape(-1, devices, minor)  22.2 us
    all_to_all x2, starting transfers between devices, exchange(): return lax.all_to_all(rows, AXES, 0, 0, tiled=True)  22.1 us
    dot_general x7, local copies, waits for them, and re-layouts, multiply(): lax.dot_general(matrix, kernel, (((0,), (0,)), ((), ())), precision=lax.P...  18.1 us
    transpose x1, local copies, waits for them, and re-layouts, exchange(): rows = jnp.transpose(shaped, (1, 0, 2)).reshape(devices, -1)  17.4 us
    mul x3, local copies, waits for them, and re-layouts, contract(): result.reshape(-1, 4, 4, spread // 4) * first_bond[None, :, :, None]  11.6 us
    all_to_all x2, other arithmetic, exchange(): return lax.all_to_all(rows, AXES, 0, 0, tiled=True)  9.72 us
  transfers between devices with their start and end apart: 2, of which 1 were waited for; matrix products, arithmetic and copies ran while one was open for 16% of the time, Pallas kernels for 0%

commit v1 on v0

--- a/solution.py
+++ b/solution.py
@@ -33,18 +33,30 @@
     )
 
 
-def contract(flat, kernel, first_bond, spread):
-    result = multiply(flat.reshape(spread, -1), kernel)
-    bonded = result.reshape(-1, 4, 4, spread // 4) * first_bond[None, :, :, None]
+def exchange(flat, devices, spread, extra=None):
+    shaped = flat.reshape(2, spread, devices, -1)
+    rows = jnp.transpose(shaped, (2, 0, 3, 1)).reshape(devices, -1)
+    if extra is not None:
+        rows = jnp.concatenate([rows, extra], axis=1)
+    return lax.all_to_all(rows, AXES, 0, 0, tiled=True)
+
+
+def contract_middle(flat, kernel, first_bond, spread, low):
+    result = lax.dot_general(
+        flat.reshape(low, spread, -1),
+        kernel,
+        (((1,), (0,)), ((), ())),
+        precision=lax.Precision.HIGHEST,
+        preferred_element_type=jnp.float32,
+    )
+    bonded = result.reshape(low, -1, 4, 4, spread // 4) * first_bond[None, None, :, :, None]
     return bonded.reshape(-1)
 
 
-def exchange(flat, devices, minor, extra=None):
-    shaped = flat.reshape(-1, devices, minor)
-    rows = jnp.transpose(shaped, (1, 0, 2)).reshape(devices, -1)
-    if extra is not None:
-        rows = jnp.concatenate([rows, extra], axis=1)
-    return lax.all_to_all(rows, AXES, 0, 0, tiled=True)
+def contract_lead(flat, kernel, first_bond, spread, low):
+    result = multiply(flat.reshape(spread, -1), kernel).reshape(low // 4, 4, -1, 4, spread // 4)
+    bonded = result * first_bond[None, :, None, :, None]
+    return bonded.reshape(-1)
 
 
 def shards(state, couplings):
@@ -54,7 +66,7 @@
     me = lax.axis_index("lead") * sub_count + lax.axis_index("sub")
     spread = 4**BLOCK
     whole_count = state.shape[0] * devices
-    minor = 4**5 // devices
+    low = 4**5 // devices
     kernels = []
     for block in range(2 * WINDOWS):
         first_site = block * BLOCK
@@ -66,9 +78,9 @@
             )
         )
 
-    current = exchange(state, devices, minor).reshape(-1)
-    current = contract(current, *kernels[0], spread)
-    current = contract(current, *kernels[1], spread)
+    current = exchange(state, devices, spread).reshape(-1)
+    current = contract_lead(current, *kernels[0], spread, low)
+    current = contract_middle(current, *kernels[1], spread, low)
 
     kernel3, bond3 = kernels[2]
     kernel4, bond4 = kernels[3]
@@ -86,13 +98,13 @@
 
     extra = jnp.zeros((devices, 128), jnp.float32)
     extra = extra.at[:, 0].set(middle_part).at[:, 1].set(final_part)
-    received = exchange(current, devices, minor, extra)
+    received = exchange(current, devices, spread, extra)
     middle_total = jnp.sum(received[:, -128])
     final_total = jnp.sum(received[:, -127])
     current = received[:, :-128].reshape(-1)
 
-    current = contract(current, *kernels[2], spread)
-    current = contract(current, *kernels[3], spread)
+    current = contract_lead(current, *kernels[2], spread, low)
+    current = contract_middle(current, *kernels[3], spread, low)
 
     middle_mean = middle_total / whole_count
     last_mean = final_total / middle_mean / whole_count

time: 235 us -> 214 us (0.911)
  local copies, waits for them, and re-layouts: 113 us -> 98.1 us
  other arithmetic: 32.6 us -> 29.2 us
    dot_general x4 -> x2, matrix products: 28.8 us -> 9.22 us  [multiply(): lax.dot_general(matrix, kernel, (((0,), (0,)), ((), ())), precision=lax.P...]
    dot_general x0 -> x2, matrix products: none -> 17.6 us  [contract_middle(): lax.dot_general(flat.reshape(low, spread, -1), kernel, (((1,), (0,)), (()...]
    dot_general x7 -> x1, local copies, waits for them, and re-layouts: 18.1 us -> 1.92 us  [multiply(): lax.dot_general(matrix, kernel, (((0,), (0,)), ((), ())), precision=lax.P...]
    mul x3 -> x4, local copies, waits for them, and re-layouts: 11.6 us -> 5.52 us  [the longest x1 5.23 us: contract_middle(): result.reshape(low, -1, 4, 4, spread // 4)]
    mul x2 -> x3, local copies, waits for them, and re-layouts: 4.81 us -> 9.35 us  [shards(): final_part = jnp.sum(current.reshape(per_row, spread, -1, 4) * weight)]
    dot_general x1 -> x0, other arithmetic: 3.88 us -> none  [multiply(): lax.dot_general(matrix, kernel, (((0,), (0,)), ((), ())), precision=lax.P...]
    transpose x1 -> x2, local copies, waits for them, and re-layouts: 17.4 us -> 20.8 us  [exchange(): rows = jnp.transpose(shaped, (2, 0, 3, 1)).reshape(devices, -1)]
    reshape x2 -> x1, local copies, waits for them, and re-layouts: 24.9 us -> 22.2 us  [exchange(): shaped = flat.reshape(2, spread, devices, -1)]
where the time goes in v1:
time: 214 us; the launch traced here: 212 us
  local copies, waits for them, and re-layouts  98.1 us (46%)
  other arithmetic  29.2 us (14%)
  matrix products  29.2 us (14%)
  waiting for transfers between devices  27.3 us (13%)
  starting transfers between devices  22.1 us (10%)
  between operations  6.62 us (3%)
    all_to_all x2, waiting for transfers between devices, exchange(): return lax.all_to_all(rows, AXES, 0, 0, tiled=True)  27.3 us
    reshape x1, local copies, waits for them, and re-layouts, exchange(): shaped = flat.reshape(2, spread, devices, -1)  22.2 us
    all_to_all x2, starting transfers between devices, exchange(): return lax.all_to_all(rows, AXES, 0, 0, tiled=True)  22.1 us
    transpose x2, local copies, waits for them, and re-layouts, exchange(): rows = jnp.transpose(shaped, (2, 0, 3, 1)).reshape(devices, -1)  20.8 us
    dot_general x2, matrix products, contract_middle(): lax.dot_general(flat.reshape(low, spread, -1), kernel, (((1,), (0,)), (()...  17.6 us
    div x2, local copies, waits for them, and re-layouts, shards(): current = current / (middle_mean * last_mean)  9.74 us
    all_to_all x2, other arithmetic, exchange(): return lax.all_to_all(rows, AXES, 0, 0, tiled=True)  9.72 us
    add x10, other arithmetic, block_kernel(): kernel = kernel * (1.0 + horizontal[level] * chained)[None, :]  9.39 us
  transfers between devices with their start and end apart: 2, of which 1 were waited for; matrix products, arithmetic and copies ran while one was open for 16% of the time, Pallas kernels for 0%

profile of v1, /device:TPU:1, one launch (start us, length us, event | category | flops | bytes accessed | tf_op | source)
XLA Modules:
  0.0 212.5 jit_solution(2047526837034513959)
XLA Ops:
  0.6 22.2 %reshape.833 = f32[2,256,128,8]{3,2,1,0:T(8,128)} reshape(f32[524288]{0:T(1024)} %param.6) | data formatting | bytes 4194304 | tf_op jit(solution)/shard_map/reshape | solution.py:37
  22.8 18.4 %copy.64 = f32[128,2,8,256]{0,3,2,1:T(8,128)S(1)} copy(f32[128,2,8,256]{2,0,3,1:T(8,128)} %bitcast.99) | data formatting | bytes 4194304 | tf_op jit(solution)/shard_map/transpose | solution.py:38
  41.2 4.0 %copy.65 = f32[128,1,4096]{2,1,0:T(1,128)} copy(f32[128,1,4096]{0,2,1:T(8,128)S(1)} %bitcast.102) | data formatting | bytes 4194304 | tf_op jit(solution)/shard_map/all_to_all | solution.py:41
  45.1 11.9 %all-to-all-start = ((f32[128,1,4096]{2,1,0:T(1,128)}), f32[128,1,4096]{2,1,0:T(1,128)}, u32[]{:S(2)}, u32[]{:S(2)}) async-start(f32[128,1,4096]{2,1,0:T(1,128)} %copy.65), calls=%async_computation | async-start | bytes 4194304 | tf_op jit(solution)/shard_map/all_to_all | solution.py:41
  60.5 2.8 %multiply_reduce_fusion.1 = f32[256,4]{0,1:T(4,128)S(1)} fusion(f32[4,64]{1,0:T(4,128)S(1)} %get-tuple-element.77, f32[4,64]{1,0:T(4,128)S(1)} %get-tuple-element.78, f32[4,64]{1,0:T(4,128)S(1)} %select_add_fusion.6, f32[]{:T(128)} %bitcast.40, s32[4,64]{1,0:T(4,128)S(1)} %get-tuple-element.73, s32[256]{0:T(256)S(1)} %get-tuple-element.65, f32[]{:T(128)} %bitcast.39, ...), kind=kLoop, calls=%fused_computation.77 | loop fusion | flops 1244160 | bytes 15376 | tf_op jit(solution)/shard_map/reduce_sum | solution.py:87
  68.1 1.3 select_add_fusion.13
  71.6 1.7 fusion.2
  73.8 3.5 %mul.707 = f32[8,64,4,4,64]{1,0,4,3,2:T(8,128)} reshape(f32[2,256,256,4]{1,0,3,2:T(2,128)S(1)} %mul.706) | data formatting | bytes 4194304 | tf_op jit(solution)/shard_map/mul | solution.py:97
  77.3 5.3 %copy.75 = f32[8,64,4,4,64]{4,1,3,2,0:T(8,128)} copy(f32[8,64,4,4,64]{1,0,4,3,2:T(8,128)} %mul.707) | data formatting | bytes 4194304 | tf_op jit(solution)/shard_map/mul | solution.py:97
  88.2 1.2 select_add_fusion.9
  89.5 8.0 %reduce.18 = f32[128,4096]{1,0:T(8,128)} reduce(f32[128,1,4096]{2,1,0:T(1,128)} %all-to-all-done, f32[]{:T(128)} %constant.403), dimensions={1}, to_apply=%all_to_all.15.reduce_sub_computation | reduce | bytes 4194308 | tf_op jit(solution)/shard_map/all_to_all | solution.py:41
  97.5 1.9 reshape_reshape.14
  99.4 4.6 %fusion.11 = f32[256,2048]{1,0:T(8,128)S(1)} fusion(f32[256,2048]{1,0:T(8,128)S(1)} %reshape_reshape.14, f32[256]{0:T(256)S(1)} %get-tuple-element.71, f32[256]{0:T(256)S(1)} %get-tuple-element.72, f32[256]{0:T(256)S(1)} %select_add_fusion.18, f32[]{:T(128)} %bitcast.3, f32[]{:T(128)} %bitcast.2, s32[256]{0:T(256)S(1)} %get-tuple-element.66, f32[]{:T(128)} %bitcast.1, ...), kind=kOutput, calls=%fused_computation.39 | convolution fusion | flops 1611792384 | bytes 4201488 | tf_op jit(solution)/shard_map/dot_general | solution.py:27
  105.3 1.8 copy-done
  107.1 10.1 %multiply_reduce_fusion = (f32[]{:T(128)}, f32[]{:T(128)}, f32[8,64,4,4,64]{4,1,3,2,0:T(8,128)}) fusion(f32[8,64,4,4,64]{4,1,3,2,0:T(8,128)S(1)} %copy-done, f32[4,4]{1,0:T(4,128)S(1)} %copy.69, f32[4,64]{1,0:T(4,128)S(1)} %get-tuple-element.79, f32[4,64]{1,0:T(4,128)S(1)} %get-tuple-element.80, f32[4,64]{1,0:T(4,128)S(1)} %select_add_fusion.11, ...), kind=kOutput, calls=%fused_computation.3 | convolution fusion | flops 1613889536 | bytes 6302808 | tf_op jit(solution)/shard_map/dot_general | solution.py:45
  117.2 5.2 %copy.70 = f32[8,64,4,4,64]{1,0,4,3,2:T(8,128)} copy(f32[8,64,4,4,64]{4,1,3,2,0:T(8,128)} %get-tuple-element.62) | data formatting | bytes 4194304 | tf_op jit(solution)/shard_map/mul | solution.py:52
  122.4 4.1 %reshape_reshape.15 = f32[2,256,128,8]{1,0,3,2:T(2,128)S(1)} reshape(f32[8,64,4,4,64]{1,0,4,3,2:T(8,128)} %copy.70) | data formatting | bytes 4194304 | tf_op jit(solution)/shard_map/reshape;reshape | solution.py:37
  126.6 2.4 %copy.71 = f32[128,2,8,256]{0,3,2,1:T(8,128)} copy(f32[128,2,8,256]{3,1,2,0:T(2,128)S(1)} %bitcast.103) | data formatting | bytes 4194304 | tf_op jit(solution)/shard_map/transpose | solution.py:38
  131.6 1.7 maximum_bitcast_fusion
  133.3 4.2 %copy.76 = f32[128,1,4224]{2,1,0:T(1,128)} copy(f32[128,1,4224]{0,2,1:T(8,128)S(1)} %maximum_bitcast_fusion) | data formatting | bytes 4325376 | tf_op jit(solution)/shard_map/all_to_all | solution.py:41
  137.5 10.2 %all-to-all-start.1 = ((f32[128,1,4224]{2,1,0:T(1,128)}), f32[128,1,4224]{2,1,0:T(1,128)}, u32[]{:S(2)}, u32[]{:S(2)}) async-start(f32[128,1,4224]{2,1,0:T(1,128)} %copy.76), calls=%async_computation.1 | async-start | bytes 4325376 | tf_op jit(solution)/shard_map/all_to_all | solution.py:41
  149.0 1.3 select_add_fusion
  150.3 27.2 %all-to-all-done.1 = f32[128,1,4224]{2,1,0:T(1,128)} async-done(((f32[128,1,4224]{2,1,0:T(1,128)}), f32[128,1,4224]{2,1,0:T(1,128)}, u32[]{:S(2)}, u32[]{:S(2)}) %all-to-all-start.1) | async-done | bytes 2162720 | tf_op jit(solution)/shard_map/all_to_all | solution.py:41
  177.6 1.7 copy.104
  182.0 1.5 slice.245
  183.6 2.8 %reshape_reshape.16 = f32[256,2048]{1,0:T(8,128)} reshape(f32[128,4096]{1,0:T(8,128)} %slice.245) | data formatting | bytes 4194304 | tf_op jit(solution)/shard_map/reshape;reshape | solution.py:57
  186.3 1.9 copy.77
  188.3 4.6 %convolution_multiply_fusion.1 = f32[2,4,256,4,64]{2,4,3,1,0:T(8,128)S(1)} fusion(f32[2,4,256,256,1]{3,2,4,1,0:T(8,128)S(1)} %bitcast.105, f32[4,4]{1,0:T(4,128)S(1)} %copy.78, f32[4,64]{1,0:T(4,128)S(1)} %get-tuple-element.81, f32[4,64]{1,0:T(4,128)S(1)} %get-tuple-element.82, f32[4,64]{1,0:T(4,128)S(1)} %select_add_fusion.2, f32[]{:T(128)} %bitcast.30, ...), kind=kOutput, calls=%fused_computation.10 | convolution fusion | flops 1612316672 | bytes 4205648 | tf_op jit(solution)/shard_map/dot_general | solution.py:27
  192.9 1.2 copy.79
  194.1 7.5 %multiply_divide_fusion = f32[8,64,4,4,64]{4,1,3,2,0:T(8,128)S(1)} fusion(f32[8,64,4,256,1]{3,0,2,1,4:T(8,128)S(1)} %bitcast.111, f32[]{:T(128)S(6)} %mul.754, f32[4,4]{1,0:T(4,128)S(1)} %copy.81, f32[4,64]{1,0:T(4,128)S(1)} %get-tuple-element.77, f32[4,64]{1,0:T(4,128)S(1)} %get-tuple-element.78, f32[4,64]{1,0:T(4,128)S(1)} %select_add_fusion.6, ...), kind=kOutput, calls=%fused_computation.2 | convolution fusion | flops 1612840960 | bytes 4205652 | tf_op jit(solution)/shard_map/dot_general | solution.py:45
  201.6 4.6 %copy.82 = f32[8,64,4,4,64]{4,3,2,1,0:T(4,128)} copy(f32[8,64,4,4,64]{4,1,3,2,0:T(8,128)S(1)} %multiply_divide_fusion) | data formatting | bytes 4194304 | tf_op jit(solution)/shard_map/div | solution.py:111
  206.2 5.1 %div.192 = f32[524288]{0:T(1024)} reshape(f32[8,64,4,4,64]{4,3,2,1,0:T(4,128)} %copy.82) | data formatting | bytes 4194304 | tf_op jit(solution)/shard_map/div | solution.py:111
  (53 shorter events, 19.8 us)
Async XLA Ops:
  45.1 12.0 %copy-start.1 = (f32[2,16]{1,0:T(2,128)S(1)}, f32[2,16]{1,0:T(2,128)}, u32[]{:S(2)}) copy-start(f32[2,16]{1,0:T(2,128)} %param.7) | copy-start | bytes 388
  45.1 44.3 %all-to-all-start = ((f32[128,1,4096]{2,1,0:T(1,128)}), f32[128,1,4096]{2,1,0:T(1,128)}, u32[]{:S(2)}, u32[]{:S(2)}) async-start(f32[128,1,4096]{2,1,0:T(1,128)} %copy.65), calls=%async_computation | async-start | bytes 4194304 | tf_op jit(solution)/shard_map/all_to_all | solution.py:41
  104.9 2.2 %copy-start = (f32[8,64,4,4,64]{4,1,3,2,0:T(8,128)S(1)}, f32[8,64,4,4,64]{4,1,3,2,0:T(8,128)}, u32[]{:S(2)}) copy-start(f32[8,64,4,4,64]{4,1,3,2,0:T(8,128)} %copy.75) | copy-start | bytes 6291460
  137.5 40.1 %all-to-all-start.1 = ((f32[128,1,4224]{2,1,0:T(1,128)}), f32[128,1,4224]{2,1,0:T(1,128)}, u32[]{:S(2)}, u32[]{:S(2)}) async-start(f32[128,1,4224]{2,1,0:T(1,128)} %copy.76), calls=%async_computation.1 | async-start | bytes 4325376 | tf_op jit(solution)/shard_map/all_to_all | solution.py:41
